TPU v7x, 256 devices: a whole 4x4x8 slice. The times are simulated.
256 devices in a mesh: grp: 32 (over z, y_hi, core), tp: 8 (over y_lo, x).
Axes of the slice: x: 4, y: 4 (y_hi: 2, y_lo: 2; y = y_hi * 2 + y_lo), z: 8, core: 2. Of those that a mesh axis runs over, the one named last changes fastest.
Arguments:
- states_in: bfloat16 [16384, 1536], P('grp', 'tp'), may hold values from -6 to 6
- segment_ids: int32 [16384], P('grp'), may hold values from 0 to 223, as said below
- positions: int32 [16384], P('grp'), may hold values from 0 to 1009, as said below
- attention_gain: bfloat16 [1536], P('tp'), may hold values from 0.5 to 1.5
- feedforward_gain: bfloat16 [1536], P('tp'), may hold values from 0.5 to 1.5
- query_weight: bfloat16 [1536, 1536], P('grp', 'tp'), may hold values from -1 to 1
- keyvalue_weight: bfloat16 [1536, 8, 128], P('grp', 'tp'), may hold values from -128 to 128
- output_weight: bfloat16 [1536, 1536], P('tp'), may hold values from -0.15625 to 0.15625
- route_experts: int32 [16384, 8], P('grp'), may hold values from 0 to 19, all different within a row; in each aligned block of 512 rows (0 to 511, 512 to 1023, ...) at most 256 rows name the same one
- route_weights: float32 [16384, 8], P('grp'), may hold values from 0.05 to 0.3
- expert_gateup: bfloat16 [40, 1536, 512], P('tp'), may hold values from -0.15625 to 0.15625
- expert_down: bfloat16 [40, 256, 1536], P('tp'), may hold values from -0.25 to 0.25
- cache_slots: int32 [16384], P('grp'), may hold values from 0 to 16383, as said below
Outputs:
- layer_output: bfloat16 [16384, 1536], P('grp', 'tp')
- paged_cache: bfloat16 [16384, 8, 128], P('grp', 'tp')
- log_sums: float32 [24, 16384], P('tp', 'grp')
Inputs may be any that keep to these rules, and one draw needn't show every extreme that they name: `segment_ids`: equal ids mark the tokens of one prompt; the tokens of a prompt lie within one pair of groups 2p and 2p+1. `positions`: positions count from 0 within each prompt; one prompt of groups 0 and 1 has 2 * (505) tokens. `route_experts`: each row names 8 different experts; at most 256 rows of one group name the same expert, and that number is reached. `cache_slots`: every cache row is named once; the tokens of each group fill exactly 16 rows of every group's block of 512 rows.
All inputs are finite; a program needn't handle non-finite values.
Results may differ from a plain program's by a relative error of at most 0.01.
The roundings to bfloat16 on the way count: a program that leaves them out, or rounds other values in their place, can miss the bound.
Values may be sent and summed in bfloat16 or wider, within the bound.
No kernel may reach another device: no remote copies, remote signals or barrier semaphores. Data moves between devices by JAX's collectives and lax.ppermute only.
A program may use at most 128 MiB of HBM per device.

v0:
```python
import jax
import jax.numpy as jnp
from jax import lax
from jax.sharding import Mesh
from jax.sharding import PartitionSpec as P

HD = 64
attn_scale = 0.015625
norm_eps = 1e-06
rope_base = 10000.0
G = ("z", "yh", "c")
T = ("yl", "x")


def rms_scale(values, gain_row):
    floats = values.astype(jnp.float32)
    mean_square = jnp.mean(floats * floats, axis=-1, keepdims=True)
    return (floats * lax.rsqrt(mean_square + norm_eps) * gain_row.astype(jnp.float32)).astype(
        jnp.bfloat16
    )


def rotate(values, places):
    half_width = values.shape[-1] // 2
    frequency = rope_base ** (-jnp.arange(half_width, dtype=jnp.float32) * 2.0 / values.shape[-1])
    angles = places.astype(jnp.float32)[:, None] * frequency[None, :]
    cosine = jnp.cos(angles)[:, None, :]
    sine_part = jnp.sin(angles)[:, None, :]
    leading = values[..., :half_width]
    trailing = values[..., half_width:]
    return jnp.concatenate(
        [leading * cosine - trailing * sine_part, trailing * cosine + leading * sine_part], axis=-1
    )


def attend_block(query_block, seg_block, pos_block, all_rows, all_seg, all_pos):
    key_part = all_rows[..., :HD]
    value_part = all_rows[..., HD:]
    scores = (
        jnp.einsum("qgrd,kgd->grqk", query_block, key_part, preferred_element_type=jnp.float32)
        * attn_scale
    )
    allowed = (seg_block[:, None] == all_seg[None, :]) & (all_pos[None, :] <= pos_block[:, None])
    masked = jnp.where(allowed, scores, -jnp.inf)
    row_peak = jnp.max(masked, axis=-1, keepdims=True)
    exponent = jnp.exp(masked - row_peak)
    row_total = jnp.sum(exponent, axis=-1, keepdims=True)
    log_total = (row_peak + jnp.log(row_total))[..., 0]
    weights_low = (exponent / row_total).astype(jnp.bfloat16)
    mixed_rows = jnp.einsum(
        "grqk,kgd->qgrd", weights_low, value_part, preferred_element_type=jnp.float32
    )
    return (mixed_rows.astype(jnp.bfloat16), log_total)


def expert_terms(normed, route_experts, route_weights, gateup, down, slot_first):
    local_experts = gateup.shape[0]
    half_units = down.shape[1]
    owned_experts = slot_first + jnp.arange(local_experts, dtype=jnp.int32)
    matches = route_experts[:, :, None] == owned_experts[None, None, :]
    route_scale = jnp.sum(jnp.where(matches, route_weights[:, :, None], 0.0), axis=1)
    gate_up = jnp.einsum("td,edf->etf", normed, gateup, preferred_element_type=jnp.float32)
    activated = (jax.nn.silu(gate_up[..., :half_units]) * gate_up[..., half_units:]).astype(
        jnp.bfloat16
    )
    produced = jnp.einsum("etf,efd->etd", activated, down, preferred_element_type=jnp.float32)
    return jnp.sum(route_scale.T[:, :, None] * produced, axis=0)


def gather_rows_over_groups(block):
    width = block.shape[1]
    nz = lax.axis_size("z")
    zi = lax.axis_index("z")
    got = [block]
    for k in range(1, nz):
        got.append(lax.ppermute(block, "z", [(i, (i + k) % nz) for i in range(nz)]))
    stacked = jnp.stack(got)
    zfull = jnp.take(stacked, (zi - jnp.arange(nz)) % nz, axis=0)
    yi = lax.axis_index("yh")
    other_y = lax.ppermute(zfull, "yh", [(0, 1), (1, 0)])
    yfull = jnp.where(yi == 0, jnp.stack([zfull, other_y]), jnp.stack([other_y, zfull]))
    ci = lax.axis_index("c")
    other_c = lax.ppermute(yfull, "c", [(0, 1), (1, 0)])
    cfull = jnp.where(ci == 0, jnp.stack([yfull, other_c]), jnp.stack([other_c, yfull]))
    return cfull.transpose(2, 1, 0, 3, 4).reshape(-1, width)


def shards(
    states_in,
    segment_ids,
    positions,
    attention_gain,
    feedforward_gain,
    query_weight,
    keyvalue_weight,
    output_weight,
    route_experts,
    route_weights,
    expert_gateup,
    expert_down,
    cache_slots,
):
    tokens = states_in.shape[0]
    width_share = states_in.shape[1]
    head_rank = lax.axis_index(T)
    group_rank = lax.axis_index(G)
    gain_rows = jnp.zeros((8, width_share), states_in.dtype)
    gain_rows = gain_rows.at[0].set(attention_gain).at[1].set(feedforward_gain)
    packed = jnp.concatenate([states_in, gain_rows], axis=0)
    packed_full = lax.all_gather(packed, T, axis=1, tiled=True)
    states_full = packed_full[:tokens]
    gain_attend = packed_full[tokens]
    gain_forward = packed_full[tokens + 1]
    normed_in = rms_scale(states_full, gain_attend)
    query_cols = query_weight.shape[1]
    keyvalue_heads = keyvalue_weight.shape[1]
    heads_local = query_cols // HD
    piece_rows = query_weight.shape[0]
    weights_packed = jnp.concatenate(
        [query_weight, keyvalue_weight.reshape(piece_rows, -1)], axis=1
    )
    weights_full = gather_rows_over_groups(weights_packed)
    query_full_w = weights_full[:, :query_cols]
    keyvalue_full_w = weights_full[:, query_cols:]
    query_sum = jnp.dot(normed_in, query_full_w, preferred_element_type=jnp.float32)
    keyvalue_sum = jnp.dot(normed_in, keyvalue_full_w, preferred_element_type=jnp.float32)
    queries = rotate(query_sum.reshape(tokens, heads_local, HD), positions).astype(jnp.bfloat16)
    keyvalue_sum = keyvalue_sum.reshape(tokens, keyvalue_heads, 2 * HD)
    key_rows = rotate(keyvalue_sum[..., :HD], positions).astype(jnp.bfloat16)
    value_rows = keyvalue_sum[..., HD:].astype(jnp.bfloat16)
    own_rows = jnp.concatenate([key_rows, value_rows], axis=-1)
    other_rows, other_seg, other_pos = lax.ppermute(
        (own_rows, segment_ids, positions), "c", [(0, 1), (1, 0)]
    )
    all_rows = jnp.concatenate([own_rows, other_rows], axis=0)
    all_seg = jnp.concatenate([segment_ids, other_seg], axis=0)
    all_pos = jnp.concatenate([positions, other_pos], axis=0)
    group_ratio = heads_local // keyvalue_heads
    query_block = queries.reshape(tokens, keyvalue_heads, group_ratio, HD)
    mixed, log_part = attend_block(query_block, segment_ids, positions, all_rows, all_seg, all_pos)
    attended = mixed.reshape(tokens, heads_local * HD)
    log_sums = log_part.reshape(heads_local, tokens)
    partial_value = jnp.dot(attended, output_weight, preferred_element_type=jnp.float32)
    summed = lax.psum(partial_value, T)
    residual = (states_full.astype(jnp.float32) + summed).astype(jnp.bfloat16)
    normed = rms_scale(residual, gain_forward)
    residual_share = lax.dynamic_slice_in_dim(residual, head_rank * width_share, width_share, 1)
    slot_first = head_rank // 2 * expert_gateup.shape[0]
    terms = expert_terms(
        normed, route_experts, route_weights, expert_gateup, expert_down, slot_first
    )
    expert_share = lax.psum_scatter(
        terms.astype(jnp.bfloat16), T, scatter_dimension=1, tiled=True
    ).astype(jnp.float32)
    layer_output = (residual_share.astype(jnp.float32) + expert_share).astype(jnp.bfloat16)
    group_count = lax.axis_size(G)
    per_owner = tokens // group_count
    owners = cache_slots // tokens
    sequence = jnp.arange(tokens, dtype=jnp.int32)
    ordering = jnp.argsort(owners * tokens + sequence)
    send_rows = own_rows[ordering].reshape(group_count, per_owner, keyvalue_heads, 2 * HD)
    send_slots = cache_slots[ordering].reshape(group_count, per_owner)
    got_rows, got_slots = (
        lax.all_to_all(send_rows, G, split_axis=0, concat_axis=0, tiled=True),
        lax.all_to_all(send_slots, G, split_axis=0, concat_axis=0, tiled=True),
    )
    targets = got_slots.reshape(tokens) - group_rank * tokens
    paged_rows = (
        jnp.zeros_like(own_rows).at[targets].set(got_rows.reshape(tokens, keyvalue_heads, 2 * HD))
    )
    return (layer_output, paged_rows, log_sums)


def solution(mesh):
    fine = Mesh(mesh.devices.reshape(8, 2, 2, 2, 4), ("z", "yh", "c", "yl", "x"))
    return jax.shard_map(
        shards,
        mesh=fine,
        in_specs=(
            P(G, T),
            P(G),
            P(G),
            P(T),
            P(T),
            P(G, T),
            P(G, T, None),
            P(T, None),
            P(G, None),
            P(G, None),
            P(T, None, None),
            P(T, None, None),
            P(G),
        ),
        out_specs=(P(G, T), P(G, T, None), P(T, G)),
        check_vma=False,
    )
```

profile of v0, /device:TPU:1, one launch (start us, length us, event | category | flops | bytes accessed | tf_op | source)
XLA Modules:
  0.0 252.0 jit_solution(752531297667724004)
XLA Ops:
  7.2 0.9 pad_maximum_fusion.3
  8.1 2.5 collective-permute-start
  10.6 3.0 %collective-permute-start.1 = (bf16[48,320]{1,0:T(8,128)(2,1)S(1)}, bf16[48,320]{1,0:T(8,128)(2,1)S(1)}, u32[]{:S(2)}, u32[]{:S(2)}) collective-permute-start(bf16[48,320]{1,0:T(8,128)(2,1)S(1)} %pad_maximum_fusion.3), channel_id=1, source_target_pairs={{0,64},{32,96},{64,128},{96,160},{128,192},{160,224},{192,0},{224,... | collective-permute-start | bytes 92168 | tf_op jit(solution)/shard_map/ppermute | solution.py:76
  13.6 3.8 %collective-permute-start.2 = (bf16[48,320]{1,0:T(8,128)(2,1)S(1)}, bf16[48,320]{1,0:T(8,128)(2,1)S(1)}, u32[]{:S(2)}, u32[]{:S(2)}) collective-permute-start(bf16[48,320]{1,0:T(8,128)(2,1)S(1)} %pad_maximum_fusion.3), channel_id=1, source_target_pairs={{0,96},{32,128},{64,160},{96,192},{128,224},{160,0},{192,32},{224,... | collective-permute-start | bytes 92168 | tf_op jit(solution)/shard_map/ppermute | solution.py:76
  17.8 0.7 reshape.415
  19.3 1.7 pad_maximum_fusion.1
  21.1 1.7 collective-permute-start.10
  22.7 0.8 bitcast_dynamic-update-slice_fusion.7
  23.6 0.7 convert_element_type.66
  24.7 4.7 %collective-permute-start.4 = (bf16[48,320]{1,0:T(8,128)(2,1)S(1)}, bf16[48,320]{1,0:T(8,128)(2,1)S(1)}, u32[]{:S(2)}, u32[]{:S(2)}) collective-permute-start(bf16[48,320]{1,0:T(8,128)(2,1)S(1)} %pad_maximum_fusion.3), channel_id=1, source_target_pairs={{0,160},{32,192},{64,224},{96,0},{128,32},{160,64},{192,96},{224,1... | collective-permute-start | bytes 92168 | tf_op jit(solution)/shard_map/ppermute | solution.py:76
  29.4 0.7 pad_add_fusion
  30.1 2.5 collective-permute-start.5
  32.6 0.8 collective-permute-start.6
  33.4 0.9 collective-permute-start.11
  34.6 0.8 collective-permute-done.6
  36.2 3.0 %collective-permute-start.7 = (bf16[8,48,320]{2,1,0:T(8,128)(2,1)S(1)}, bf16[8,48,320]{2,1,0:T(8,128)(2,1)S(1)}, u32[]{:S(2)}, u32[]{:S(2)}) collective-permute-start(bf16[8,48,320]{2,1,0:T(8,128)(2,1)S(1)} %broadcast_select_fusion), channel_id=1, source_target_pairs={{0,16},{16,0},{1,17},{17,1},{2,18},{18,2},{3,19},{19,3},{4,20},{20... | collective-permute-start | bytes 737288 | tf_op jit(solution)/shard_map/ppermute | solution.py:80
  39.2 0.7 pad_add_fusion.1
  40.0 23.9 %collective-permute-done.7 = bf16[8,48,320]{2,1,0:T(8,128)(2,1)S(1)} collective-permute-done((bf16[8,48,320]{2,1,0:T(8,128)(2,1)S(1)}, bf16[8,48,320]{2,1,0:T(8,128)(2,1)S(1)}, u32[]{:S(2)}, u32[]{:S(2)}) %collective-permute-start.7) | collective-permute-done | bytes 245792 | tf_op jit(solution)/shard_map/ppermute | solution.py:80
  64.1 0.8 collective-permute-start.8
  64.8 0.8 compare_and_fusion
  66.8 1.1 copy.50
  68.0 2.6 %slice.95 = bf16[512,1536]{0,1:T(8,128)(2,1)} slice(bf16[520,1536]{0,1:T(8,128)(2,1)} %all-gather.2.cloned.1.call-done), slice={[0:512], [0:1536]} | slice | bytes 3145728 | tf_op jit(solution)/shard_map/slice | solution.py:111
  70.6 1.7 copy.59
  72.7 1.5 convert_reduce_fusion
  74.3 2.0 convolution_bitcast_fusion.1
  76.6 0.8 fusion.22
  78.0 0.9 collective-permute-done.9
  78.9 1.3 fusion.1
  80.2 1.4 fusion
  81.6 2.0 fusion.19
  83.7 2.3 fusion.54
  86.5 91.7 %all-reduce.3.cloned.1.call-done = f32[512,1536]{1,0:T(8,128)} async-done(((f32[512,1536]{1,0:T(8,128)}), f32[512,1536]{1,0:T(8,128)}) %all-reduce.3.cloned.1.call-update) | async-done | bytes 3145744 | tf_op jit(solution)/shard_map/psum | solution.py:144
  178.2 2.4 fusion.2
  180.6 7.5 %convolution_bitcast_fusion = f32[5,512,512]{2,1,0:T(8,128)S(1)} fusion(bf16[5,1536,512]{2,1,0:T(8,128)(2,1)} %param.27, bf16[512,1536]{1,0:T(8,128)(2,1)S(1)} %get-tuple-element.47, f32[1536]{0:T(1024)S(1)} %get-tuple-element.44, f32[512]{0:T(512)S(1)} %add_rsqrt_fusion), kind=kOutput, calls=%fused_computation.26 | convolution fusion | flops 4029677568 | bytes 14688256 | tf_op jit(solution)/shard_map/td,edf->etf/dot_general | solution.py:62
  188.2 3.5 %multiply_reduce_fusion = bf16[512,1536]{1,0:T(8,128)(2,1)S(1)} fusion(bf16[5,256,1536]{2,1,0:T(8,128)(2,1)S(1)} %copy-done.8, f32[5,512]{1,0:T(8,128)S(1)} %bitcast.103, f32[5,512,512]{2,1,0:T(8,128)S(1)} %convolution_bitcast_fusion), kind=kOutput, calls=%fused_computation.4 | convolution fusion | flops 2024275968 | bytes 10758144 | tf_op jit(solution)/shard_map/etf,efd->etd/dot_general | solution.py:66
  191.7 1.6 copy.57
  193.3 3.8 %sort.17 = (s32[512]{0:T(512)}, s32[512]{0:T(512)S(1)}) sort(s32[512]{0:T(512)S(1)} %fusion.43, s32[512]{0:T(512)S(1)} %iota.31), dimensions={0}, to_apply=%region_8.9 | sort | flops 4608 | bytes 8192 | tf_op jit(solution)/shard_map/jit(argsort)/sort | solution.py:160
  197.1 3.5 %gather_fusion.1 = s32[512]{0:T(512)S(1)} fusion(s32[512]{0:T(512)S(1)} %copy-done.1, s32[1024]{0:T(1024)S(1)} %pad_clamp_fusion), kind=kCustom, calls=%fused_computation.1 | custom fusion | bytes 6144 | tf_op jit(solution)/shard_map/gather | solution.py:162
  200.6 0.7 all_to_all.9
  201.3 12.2 %all-to-all-start = ((s32[32,1,16]{2,1,0:T(1,128)}), s32[32,1,16]{2,1,0:T(1,128)S(1)}, u32[]{:S(2)}, u32[]{:S(2)}) async-start(s32[32,1,16]{2,1,0:T(1,128)} %bitcast.32), calls=%async_computation | async-start | bytes 32768 | tf_op jit(solution)/shard_map/all_to_all | solution.py:165
  213.5 9.3 %all-to-all-done = s32[32,1,16]{2,1,0:T(1,128)S(1)} async-done(((s32[32,1,16]{2,1,0:T(1,128)}), s32[32,1,16]{2,1,0:T(1,128)S(1)}, u32[]{:S(2)}, u32[]{:S(2)}) %all-to-all-start) | async-done | bytes 2080 | tf_op jit(solution)/shard_map/all_to_all | solution.py:165
  223.1 1.9 gather_fusion.2
  225.0 4.1 %all-to-all-start.1 = ((bf16[32,16,1,128]{3,1,2,0:T(8,128)(2,1)}), bf16[32,16,1,128]{3,1,2,0:T(8,128)(2,1)S(1)}, u32[]{:S(2)}, u32[]{:S(2)}) async-start(bf16[32,16,1,128]{3,1,2,0:T(8,128)(2,1)} %bitcast.36), calls=%async_computation.1 | async-start | bytes 262144 | tf_op jit(solution)/shard_map/all_to_all | solution.py:164
  229.8 10.3 %all-to-all-done.1 = bf16[32,16,1,128]{3,1,2,0:T(8,128)(2,1)S(1)} async-done(((bf16[32,16,1,128]{3,1,2,0:T(8,128)(2,1)}), bf16[32,16,1,128]{3,1,2,0:T(8,128)(2,1)S(1)}, u32[]{:S(2)}, u32[]{:S(2)}) %all-to-all-start.1) | async-done | bytes 131104 | tf_op jit(solution)/shard_map/all_to_all | solution.py:164
  240.1 2.4 scatter_custom_fusion
  242.5 1.1 copy.58
  243.5 1.2 add_convert_fusion
  244.7 0.8 copy.55
  (79 shorter events, 6.8 us)
Async XLA Ops:
  7.2 76.5 %copy-start = (bf16[192,1536]{1,0:T(8,128)(2,1)S(1)}, bf16[192,1536]{1,0:T(8,128)(2,1)}, u32[]{:S(2)}) copy-start(bf16[192,1536]{1,0:T(8,128)(2,1)} %param.24) | copy-start | bytes 1769476
  7.2 57.7 %copy-start.7 = (s32[512]{0:T(512)S(1)}, s32[512]{0:T(512)}, u32[]{:S(2)}) copy-start(s32[512]{0:T(512)} %param.18) | copy-start | bytes 6148
  7.2 57.7 %copy-start.4 = (s32[512]{0:T(512)S(1)}, s32[512]{0:T(512)}, u32[]{:S(2)}) copy-start(s32[512]{0:T(512)} %param.19) | copy-start | bytes 6148
  7.2 60.8 %all-gather.2.cloned.1.call-start = ((), (), s32[]{:S(2)}) async-start(), calls=%async_computation.3 | async-start | bytes 2211840 | tf_op jit(solution)/shard_map/all_gather | solution.py:110
  8.1 22.0 %collective-permute-start = (bf16[48,320]{1,0:T(8,128)(2,1)S(1)}, bf16[48,320]{1,0:T(8,128)(2,1)S(1)}, u32[]{:S(2)}, u32[]{:S(2)}) collective-permute-start(bf16[48,320]{1,0:T(8,128)(2,1)S(1)} %pad_maximum_fusion.3), channel_id=1, source_target_pairs={{0,32},{32,64},{64,96},{96,128},{128,160},{160,192},{192,224},{224... | collective-permute-start | bytes 92168 | tf_op jit(solution)/shard_map/ppermute | solution.py:76
  10.6 21.9 %collective-permute-start.1 = (bf16[48,320]{1,0:T(8,128)(2,1)S(1)}, bf16[48,320]{1,0:T(8,128)(2,1)S(1)}, u32[]{:S(2)}, u32[]{:S(2)}) collective-permute-start(bf16[48,320]{1,0:T(8,128)(2,1)S(1)} %pad_maximum_fusion.3), channel_id=1, source_target_pairs={{0,64},{32,96},{64,128},{96,160},{128,192},{160,224},{192,0},{224,... | collective-permute-start | bytes 92168 | tf_op jit(solution)/shard_map/ppermute | solution.py:76
  13.6 19.8 %collective-permute-start.2 = (bf16[48,320]{1,0:T(8,128)(2,1)S(1)}, bf16[48,320]{1,0:T(8,128)(2,1)S(1)}, u32[]{:S(2)}, u32[]{:S(2)}) collective-permute-start(bf16[48,320]{1,0:T(8,128)(2,1)S(1)} %pad_maximum_fusion.3), channel_id=1, source_target_pairs={{0,96},{32,128},{64,160},{96,192},{128,224},{160,0},{192,32},{224,... | collective-permute-start | bytes 92168 | tf_op jit(solution)/shard_map/ppermute | solution.py:76
  17.4 17.0 %collective-permute-start.3 = (bf16[48,320]{1,0:T(8,128)(2,1)S(1)}, bf16[48,320]{1,0:T(8,128)(2,1)S(1)}, u32[]{:S(2)}, u32[]{:S(2)}) collective-permute-start(bf16[48,320]{1,0:T(8,128)(2,1)S(1)} %pad_maximum_fusion.3), channel_id=1, source_target_pairs={{0,128},{32,160},{64,192},{96,224},{128,0},{160,32},{192,64},{224,... | collective-permute-start | bytes 92168 | tf_op jit(solution)/shard_map/ppermute | solution.py:76
  21.0 157.2 %all-reduce.3.cloned.1.call-start = ((), (), s32[]{:S(2)}) async-start(), calls=%async_computation.4 | async-start | bytes 6291456 | tf_op jit(solution)/shard_map/psum | solution.py:144
  21.1 3.6 %collective-permute-start.10 = (s32[512]{0:T(512)}, s32[512]{0:T(512)S(1)}, u32[]{:S(2)}, u32[]{:S(2)}) collective-permute-start(s32[512]{0:T(512)} %param.18), channel_id=1, source_target_pairs={{0,8},{8,0},{1,9},{9,1},{2,10},{10,2},{3,11},{11,3},{4,12},{12,4},... | collective-permute-start | bytes 6152 | tf_op jit(solution)/shard_map/ppermute | solution.py:132
  24.7 9.7 %collective-permute-start.4 = (bf16[48,320]{1,0:T(8,128)(2,1)S(1)}, bf16[48,320]{1,0:T(8,128)(2,1)S(1)}, u32[]{:S(2)}, u32[]{:S(2)}) collective-permute-start(bf16[48,320]{1,0:T(8,128)(2,1)S(1)} %pad_maximum_fusion.3), channel_id=1, source_target_pairs={{0,160},{32,192},{64,224},{96,0},{128,32},{160,64},{192,96},{224,1... | collective-permute-start | bytes 92168 | tf_op jit(solution)/shard_map/ppermute | solution.py:76
  30.1 4.5 %collective-permute-start.5 = (bf16[48,320]{1,0:T(8,128)(2,1)S(1)}, bf16[48,320]{1,0:T(8,128)(2,1)S(1)}, u32[]{:S(2)}, u32[]{:S(2)}) collective-permute-start(bf16[48,320]{1,0:T(8,128)(2,1)S(1)} %pad_maximum_fusion.3), channel_id=1, source_target_pairs={{0,192},{32,224},{64,0},{96,32},{128,64},{160,96},{192,128},{224,1... | collective-permute-start | bytes 92168 | tf_op jit(solution)/shard_map/ppermute | solution.py:76
  32.6 2.9 %collective-permute-start.6 = (bf16[48,320]{1,0:T(8,128)(2,1)S(1)}, bf16[48,320]{1,0:T(8,128)(2,1)S(1)}, u32[]{:S(2)}, u32[]{:S(2)}) collective-permute-start(bf16[48,320]{1,0:T(8,128)(2,1)S(1)} %pad_maximum_fusion.3), channel_id=1, source_target_pairs={{0,224},{32,0},{64,32},{96,64},{128,96},{160,128},{192,160},{224,1... | collective-permute-start | bytes 92168 | tf_op jit(solution)/shard_map/ppermute | solution.py:76
  33.4 5.8 %collective-permute-start.11 = (s32[512]{0:T(512)}, s32[512]{0:T(512)S(1)}, u32[]{:S(2)}, u32[]{:S(2)}) collective-permute-start(s32[512]{0:T(512)} %param.19), channel_id=1, source_target_pairs={{0,8},{8,0},{1,9},{9,1},{2,10},{10,2},{3,11},{11,3},{4,12},{12,4},... | collective-permute-start | bytes 6152 | tf_op jit(solution)/shard_map/ppermute | solution.py:132
  36.2 27.7 %collective-permute-start.7 = (bf16[8,48,320]{2,1,0:T(8,128)(2,1)S(1)}, bf16[8,48,320]{2,1,0:T(8,128)(2,1)S(1)}, u32[]{:S(2)}, u32[]{:S(2)}) collective-permute-start(bf16[8,48,320]{2,1,0:T(8,128)(2,1)S(1)} %broadcast_select_fusion), channel_id=1, source_target_pairs={{0,16},{16,0},{1,17},{17,1},{2,18},{18,2},{3,19},{19,3},{4,20},{20... | collective-permute-start | bytes 737288 | tf_op jit(solution)/shard_map/ppermute | solution.py:80
  64.1 2.4 collective-permute-start.8
  72.3 4.3 %copy-start.3 = (bf16[8,2,2,48,320]{4,3,2,1,0:T(8,128)(2,1)S(1)}, bf16[8,2,2,48,320]{4,3,2,1,0:T(8,128)(2,1)}, u32[]{:S(2)}) copy-start(bf16[8,2,2,48,320]{4,3,2,1,0:T(8,128)(2,1)} %copy.50) | copy-start | bytes 2949124
  77.5 1.4 collective-permute-start.9
  83.7 2.7 %copy-start.5 = (f32[512,8]{0,1:T(8,128)S(1)}, f32[512,8]{0,1:T(8,128)}, u32[]{:S(2)}) copy-start(f32[512,8]{0,1:T(8,128)} %param.26) | copy-start | bytes 49156
  83.7 2.7 %copy-start.6 = (s32[512,8]{0,1:T(8,128)S(1)}, s32[512,8]{0,1:T(8,128)}, u32[]{:S(2)}) copy-start(s32[512,8]{0,1:T(8,128)} %param.25) | copy-start | bytes 49156
  86.0 156.4 %reduce-scatter.4.cloned.1.call-start = ((), (), s32[]{:S(2)}) async-start(), calls=%async_computation.5 | async-start | bytes 1769472
  180.6 7.6 %copy-start.2 = (bf16[512,1536]{1,0:T(8,128)(2,1)}, bf16[512,1536]{1,0:T(8,128)(2,1)S(1)}, u32[]{:S(2)}) copy-start(bf16[512,1536]{1,0:T(8,128)(2,1)S(1)} %get-tuple-element.47) | copy-start | bytes 4718596
  180.6 7.6 %copy-start.8 = (bf16[5,256,1536]{2,1,0:T(8,128)(2,1)S(1)}, bf16[5,256,1536]{2,1,0:T(8,128)(2,1)}, u32[]{:S(2)}) copy-start(bf16[5,256,1536]{2,1,0:T(8,128)(2,1)} %param.28) | copy-start | bytes 11796484
  191.7 1.6 copy-start.1
  201.3 21.6 %all-to-all-start = ((s32[32,1,16]{2,1,0:T(1,128)}), s32[32,1,16]{2,1,0:T(1,128)S(1)}, u32[]{:S(2)}, u32[]{:S(2)}) async-start(s32[32,1,16]{2,1,0:T(1,128)} %bitcast.32), calls=%async_computation | async-start | bytes 32768 | tf_op jit(solution)/shard_map/all_to_all | solution.py:165
  225.0 15.1 %all-to-all-start.1 = ((bf16[32,16,1,128]{3,1,2,0:T(8,128)(2,1)}), bf16[32,16,1,128]{3,1,2,0:T(8,128)(2,1)S(1)}, u32[]{:S(2)}, u32[]{:S(2)}) async-start(bf16[32,16,1,128]{3,1,2,0:T(8,128)(2,1)} %bitcast.36), calls=%async_computation.1 | async-start | bytes 262144 | tf_op jit(solution)/shard_map/all_to_all | solution.py:164
Sparse Core Ops, SparseCore 0:
  21.1 40.3 all-gather.1
  86.2 91.9 all-reduce.2
  193.4 40.6 reduce-scatter.3
where the time goes:
time: 253 us; the launch traced here: 252 us
  waiting for transfers between devices  138 us (55%)
  starting transfers between devices  41.3 us (16%)
  local copies, waits for them, and re-layouts  19.8 us (8%)
  other arithmetic  19.5 us (8%)
  matrix products  19.4 us (8%)
  between operations  14.2 us (6%)
    psum x1, waiting for transfers between devices, shards(): summed = lax.psum(partial_value, T)  91.7 us
    ppermute x1, waiting for transfers between devices, gather_rows_over_groups(): other_y = lax.ppermute(zfull, 'yh', [(0, 1), (1, 0)])  23.9 us
    ppermute x7, starting transfers between devices, gather_rows_over_groups(): got.append(lax.ppermute(block, 'z', [(i, (i + k) % nz) for i in range(nz)]))  17.7 us
    all_to_all x1, starting transfers between devices, shards(): lax.all_to_all(send_slots, G, split_axis=0, concat_axis=0, tiled=True)  12.2 us
    all_to_all x1, waiting for transfers between devices, shards(): lax.all_to_all(send_rows, G, split_axis=0, concat_axis=0, tiled=True)  10.3 us
    all_to_all x1, waiting for transfers between devices, shards(): lax.all_to_all(send_slots, G, split_axis=0, concat_axis=0, tiled=True)  9.3 us
    dot_general x1, matrix products, expert_terms(): jnp.einsum('td,edf->etf', normed, gateup, preferred_element_type=jnp.floa...  7.52 us
    unnamed x28, local copies, waits for them, and re-layouts  5.28 us
  transfers between devices with their start and end apart: 17, of which 8 were waited for; matrix products, arithmetic and copies ran while one was open for 9% of the time, Pallas kernels for 0%

commit v1 on v0

--- a/solution.py
+++ b/solution.py
@@ -10,6 +10,9 @@
 rope_base = 10000.0
 G = ("z", "yh", "c")
 T = ("yl", "x")
+update_tasks = lambda block_in, device_axis, mesh_dim: lax.psum(
+    lax.psum(block_in, axis_name=device_axis), axis_name=mesh_dim
+)
 
 
 def rms_scale(values, gain_row):
@@ -141,7 +144,7 @@
     attended = mixed.reshape(tokens, heads_local * HD)
     log_sums = log_part.reshape(heads_local, tokens)
     partial_value = jnp.dot(attended, output_weight, preferred_element_type=jnp.float32)
-    summed = lax.psum(partial_value, T)
+    summed = update_tasks(partial_value, "x", "yl")
     residual = (states_full.astype(jnp.float32) + summed).astype(jnp.bfloat16)
     normed = rms_scale(residual, gain_forward)
     residual_share = lax.dynamic_slice_in_dim(residual, head_rank * width_share, width_share, 1)

time: 253 us -> 338 us (1.34)
  waiting for transfers between devices: 138 us -> 225 us
    psum x1 -> x2, waiting for transfers between devices: 91.7 us -> 179 us  [the longest x1 99.6 us: lax.psum(lax.psum(block_in, axis_name=device_axis), axis_name=mesh_dim)]
  transfers between devices with their start and end apart: 17 -> 18, of which waited for: 8 -> 9; matrix products, arithmetic and copies ran while one was open for 9% -> 7% of each run, Pallas kernels for 0% -> 0%
where the time goes in v1:
time: 338 us; the launch traced here: 337 us
  waiting for transfers between devices  225 us (67%)
  starting transfers between devices  39.1 us (12%)
  local copies, waits for them, and re-layouts  19.8 us (6%)
  other arithmetic  19.5 us (6%)
  matrix products  19.4 us (6%)
  between operations  14.2 us (4%)
    psum x1, waiting for transfers between devices, lax.psum(lax.psum(block_in, axis_name=device_axis), axis_name=mesh_dim)  99.6 us
    psum x1, waiting for transfers between devices, lax.psum(block_in, axis_name=device_axis)  79.6 us
    ppermute x1, waiting for transfers between devices, gather_rows_over_groups(): other_y = lax.ppermute(zfull, 'yh', [(0, 1), (1, 0)])  23.9 us
    ppermute x7, starting transfers between devices, gather_rows_over_groups(): got.append(lax.ppermute(block, 'z', [(i, (i + k) % nz) for i in range(nz)]))  17.7 us
    all_to_all x1, waiting for transfers between devices, shards(): lax.all_to_all(send_rows, G, split_axis=0, concat_axis=0, tiled=True)  10.4 us
    all_to_all x1, starting transfers between devices, shards(): lax.all_to_all(send_slots, G, split_axis=0, concat_axis=0, tiled=True)  9.99 us
    all_to_all x1, waiting for transfers between devices, shards(): lax.all_to_all(send_slots, G, split_axis=0, concat_axis=0, tiled=True)  9.28 us
    dot_general x1, matrix products, expert_terms(): jnp.einsum('td,edf->etf', normed, gateup, preferred_element_type=jnp.floa...  7.51 us
  transfers between devices with their start and end apart: 18, of which 9 were waited for; matrix products, arithmetic and copies ran while one was open for 7% of the time, Pallas kernels for 0%

profile of v1, /device:TPU:1, one launch (start us, length us, event | category | flops | bytes accessed | tf_op | source)
XLA Modules:
  0.0 337.2 jit_solution(14730869390227129197)
XLA Ops:
  7.2 0.9 pad_maximum_fusion.3
  8.1 2.5 collective-permute-start
  10.6 3.0 collective-permute-start.1
  13.6 3.8 %collective-permute-start.2 = (bf16[48,320]{1,0:T(8,128)(2,1)S(1)}, bf16[48,320]{1,0:T(8,128)(2,1)S(1)}, u32[]{:S(2)}, u32[]{:S(2)}) collective-permute-start(bf16[48,320]{1,0:T(8,128)(2,1)S(1)} %pad_maximum_fusion.3), channel_id=1, source_target_pairs={{0,96},{32,128},{64,160},{96,192},{128,224},{160,0},{192,32},{224,... | collective-permute-start | bytes 92168 | tf_op jit(solution)/shard_map/ppermute | solution.py:79
  19.3 1.7 pad_maximum_fusion.1
  21.1 1.7 collective-permute-start.10
  22.7 0.8 bitcast_dynamic-update-slice_fusion.7
  23.6 0.7 convert_element_type.66
  24.7 4.7 %collective-permute-start.4 = (bf16[48,320]{1,0:T(8,128)(2,1)S(1)}, bf16[48,320]{1,0:T(8,128)(2,1)S(1)}, u32[]{:S(2)}, u32[]{:S(2)}) collective-permute-start(bf16[48,320]{1,0:T(8,128)(2,1)S(1)} %pad_maximum_fusion.3), channel_id=1, source_target_pairs={{0,160},{32,192},{64,224},{96,0},{128,32},{160,64},{192,96},{224,1... | collective-permute-start | bytes 92168 | tf_op jit(solution)/shard_map/ppermute | solution.py:79
  29.4 0.7 pad_add_fusion
  30.1 2.5 collective-permute-start.5
  32.6 0.8 collective-permute-start.6
  33.4 0.9 collective-permute-start.11
  34.6 0.8 collective-permute-done.6
  36.2 3.0 collective-permute-start.7
  39.2 0.7 pad_add_fusion.1
  40.0 23.9 %collective-permute-done.7 = bf16[8,48,320]{2,1,0:T(8,128)(2,1)S(1)} collective-permute-done((bf16[8,48,320]{2,1,0:T(8,128)(2,1)S(1)}, bf16[8,48,320]{2,1,0:T(8,128)(2,1)S(1)}, u32[]{:S(2)}, u32[]{:S(2)}) %collective-permute-start.7) | collective-permute-done | bytes 245792 | tf_op jit(solution)/shard_map/ppermute | solution.py:83
  64.1 0.8 collective-permute-start.8
  64.8 0.8 compare_and_fusion
  66.8 1.1 copy.50
  68.0 2.6 slice.95
  70.6 1.7 copy.59
  72.7 1.5 convert_reduce_fusion
  74.3 2.0 convolution_bitcast_fusion.1
  76.6 0.8 fusion.22
  78.0 0.9 collective-permute-done.9
  78.9 1.3 fusion.1
  80.2 1.4 fusion
  81.6 2.0 fusion.19
  83.7 2.3 fusion.54
  86.1 79.6 %all-reduce.4.cloned.1.call-done = f32[512,1536]{1,0:T(8,128)} async-done(((f32[512,1536]{1,0:T(8,128)}), f32[512,1536]{1,0:T(8,128)}) %all-reduce.4.cloned.1.call-update) | async-done | bytes 3145744 | tf_op jit(solution)/shard_map/psum | solution.py:14
  166.1 99.6 %all-reduce.6.cloned.1.call-done = f32[512,1536]{1,0:T(8,128)} async-done(((f32[512,1536]{1,0:T(8,128)}), f32[512,1536]{1,0:T(8,128)}) %all-reduce.6.cloned.1.call-update) | async-done | bytes 3145744 | tf_op jit(solution)/shard_map/psum | solution.py:13
  265.7 2.4 fusion.2
  268.1 7.5 %convolution_bitcast_fusion = f32[5,512,512]{2,1,0:T(8,128)S(1)} fusion(bf16[5,1536,512]{2,1,0:T(8,128)(2,1)} %param.27, bf16[512,1536]{1,0:T(8,128)(2,1)S(1)} %get-tuple-element.47, f32[1536]{0:T(1024)S(1)} %get-tuple-element.44, f32[512]{0:T(512)S(1)} %add_rsqrt_fusion), kind=kOutput, calls=%fused_computation.26 | convolution fusion | flops 4029677568 | bytes 14688256 | tf_op jit(solution)/shard_map/td,edf->etf/dot_general | solution.py:65
  275.6 3.5 %multiply_reduce_fusion = bf16[512,1536]{1,0:T(8,128)(2,1)S(1)} fusion(bf16[5,256,1536]{2,1,0:T(8,128)(2,1)S(1)} %copy-done.8, f32[5,512]{1,0:T(8,128)S(1)} %bitcast.103, f32[5,512,512]{2,1,0:T(8,128)S(1)} %convolution_bitcast_fusion), kind=kOutput, calls=%fused_computation.4 | convolution fusion | flops 2024275968 | bytes 10758144 | tf_op jit(solution)/shard_map/etf,efd->etd/dot_general | solution.py:69
  279.1 1.6 copy.57
  280.8 3.8 %sort.17 = (s32[512]{0:T(512)}, s32[512]{0:T(512)S(1)}) sort(s32[512]{0:T(512)S(1)} %fusion.43, s32[512]{0:T(512)S(1)} %iota.31), dimensions={0}, to_apply=%region_9.10 | sort | flops 4608 | bytes 8192 | tf_op jit(solution)/shard_map/jit(argsort)/sort | solution.py:163
  284.6 3.5 %gather_fusion.1 = s32[512]{0:T(512)S(1)} fusion(s32[512]{0:T(512)S(1)} %copy-done.1, s32[1024]{0:T(1024)S(1)} %pad_clamp_fusion), kind=kCustom, calls=%fused_computation.1 | custom fusion | bytes 6144 | tf_op jit(solution)/shard_map/gather | solution.py:165
  288.1 0.7 all_to_all.9
  288.8 10.0 %all-to-all-start = ((s32[32,1,16]{2,1,0:T(1,128)}), s32[32,1,16]{2,1,0:T(1,128)S(1)}, u32[]{:S(2)}, u32[]{:S(2)}) async-start(s32[32,1,16]{2,1,0:T(1,128)} %bitcast.32), calls=%async_computation | async-start | bytes 32768 | tf_op jit(solution)/shard_map/all_to_all | solution.py:168
  298.8 9.3 %all-to-all-done = s32[32,1,16]{2,1,0:T(1,128)S(1)} async-done(((s32[32,1,16]{2,1,0:T(1,128)}), s32[32,1,16]{2,1,0:T(1,128)S(1)}, u32[]{:S(2)}, u32[]{:S(2)}) %all-to-all-start) | async-done | bytes 2080 | tf_op jit(solution)/shard_map/all_to_all | solution.py:168
  308.3 1.9 gather_fusion.2
  310.2 4.1 %all-to-all-start.1 = ((bf16[32,16,1,128]{3,1,2,0:T(8,128)(2,1)}), bf16[32,16,1,128]{3,1,2,0:T(8,128)(2,1)S(1)}, u32[]{:S(2)}, u32[]{:S(2)}) async-start(bf16[32,16,1,128]{3,1,2,0:T(8,128)(2,1)} %bitcast.36), calls=%async_computation.1 | async-start | bytes 262144 | tf_op jit(solution)/shard_map/all_to_all | solution.py:167
  315.0 10.4 %all-to-all-done.1 = bf16[32,16,1,128]{3,1,2,0:T(8,128)(2,1)S(1)} async-done(((bf16[32,16,1,128]{3,1,2,0:T(8,128)(2,1)}), bf16[32,16,1,128]{3,1,2,0:T(8,128)(2,1)S(1)}, u32[]{:S(2)}, u32[]{:S(2)}) %all-to-all-start.1) | async-done | bytes 131104 | tf_op jit(solution)/shard_map/all_to_all | solution.py:167
  325.3 2.4 scatter_custom_fusion
  327.7 1.1 copy.58
  328.7 1.2 add_convert_fusion
  329.9 0.8 copy.55
  (82 shorter events, 7.5 us)
Async XLA Ops:
  7.2 76.5 %copy-start = (bf16[192,1536]{1,0:T(8,128)(2,1)S(1)}, bf16[192,1536]{1,0:T(8,128)(2,1)}, u32[]{:S(2)}) copy-start(bf16[192,1536]{1,0:T(8,128)(2,1)} %param.24) | copy-start | bytes 1769476
  7.2 57.7 %copy-start.7 = (s32[512]{0:T(512)S(1)}, s32[512]{0:T(512)}, u32[]{:S(2)}) copy-start(s32[512]{0:T(512)} %param.18) | copy-start | bytes 6148
  7.2 57.7 %copy-start.4 = (s32[512]{0:T(512)S(1)}, s32[512]{0:T(512)}, u32[]{:S(2)}) copy-start(s32[512]{0:T(512)} %param.19) | copy-start | bytes 6148
  7.2 60.8 %all-gather.2.cloned.1.call-start = ((), (), s32[]{:S(2)}) async-start(), calls=%async_computation.3 | async-start | bytes 2211840 | tf_op jit(solution)/shard_map/all_gather | solution.py:113
  8.1 22.0 %collective-permute-start = (bf16[48,320]{1,0:T(8,128)(2,1)S(1)}, bf16[48,320]{1,0:T(8,128)(2,1)S(1)}, u32[]{:S(2)}, u32[]{:S(2)}) collective-permute-start(bf16[48,320]{1,0:T(8,128)(2,1)S(1)} %pad_maximum_fusion.3), channel_id=1, source_target_pairs={{0,32},{32,64},{64,96},{96,128},{128,160},{160,192},{192,224},{224... | collective-permute-start | bytes 92168 | tf_op jit(solution)/shard_map/ppermute | solution.py:79
  10.6 21.9 %collective-permute-start.1 = (bf16[48,320]{1,0:T(8,128)(2,1)S(1)}, bf16[48,320]{1,0:T(8,128)(2,1)S(1)}, u32[]{:S(2)}, u32[]{:S(2)}) collective-permute-start(bf16[48,320]{1,0:T(8,128)(2,1)S(1)} %pad_maximum_fusion.3), channel_id=1, source_target_pairs={{0,64},{32,96},{64,128},{96,160},{128,192},{160,224},{192,0},{224,... | collective-permute-start | bytes 92168 | tf_op jit(solution)/shard_map/ppermute | solution.py:79
  13.6 19.8 %collective-permute-start.2 = (bf16[48,320]{1,0:T(8,128)(2,1)S(1)}, bf16[48,320]{1,0:T(8,128)(2,1)S(1)}, u32[]{:S(2)}, u32[]{:S(2)}) collective-permute-start(bf16[48,320]{1,0:T(8,128)(2,1)S(1)} %pad_maximum_fusion.3), channel_id=1, source_target_pairs={{0,96},{32,128},{64,160},{96,192},{128,224},{160,0},{192,32},{224,... | collective-permute-start | bytes 92168 | tf_op jit(solution)/shard_map/ppermute | solution.py:79
  17.4 17.0 %collective-permute-start.3 = (bf16[48,320]{1,0:T(8,128)(2,1)S(1)}, bf16[48,320]{1,0:T(8,128)(2,1)S(1)}, u32[]{:S(2)}, u32[]{:S(2)}) collective-permute-start(bf16[48,320]{1,0:T(8,128)(2,1)S(1)} %pad_maximum_fusion.3), channel_id=1, source_target_pairs={{0,128},{32,160},{64,192},{96,224},{128,0},{160,32},{192,64},{224,... | collective-permute-start | bytes 92168 | tf_op jit(solution)/shard_map/ppermute | solution.py:79
  21.0 144.6 %all-reduce.4.cloned.1.call-start = ((), (), s32[]{:S(2)}) async-start(), calls=%async_computation.4 | async-start | bytes 6291456 | tf_op jit(solution)/shard_map/psum | solution.py:14
  21.1 3.6 %collective-permute-start.10 = (s32[512]{0:T(512)}, s32[512]{0:T(512)S(1)}, u32[]{:S(2)}, u32[]{:S(2)}) collective-permute-start(s32[512]{0:T(512)} %param.18), channel_id=1, source_target_pairs={{0,8},{8,0},{1,9},{9,1},{2,10},{10,2},{3,11},{11,3},{4,12},{12,4},... | collective-permute-start | bytes 6152 | tf_op jit(solution)/shard_map/ppermute | solution.py:135
  24.7 9.7 %collective-permute-start.4 = (bf16[48,320]{1,0:T(8,128)(2,1)S(1)}, bf16[48,320]{1,0:T(8,128)(2,1)S(1)}, u32[]{:S(2)}, u32[]{:S(2)}) collective-permute-start(bf16[48,320]{1,0:T(8,128)(2,1)S(1)} %pad_maximum_fusion.3), channel_id=1, source_target_pairs={{0,160},{32,192},{64,224},{96,0},{128,32},{160,64},{192,96},{224,1... | collective-permute-start | bytes 92168 | tf_op jit(solution)/shard_map/ppermute | solution.py:79
  30.1 4.5 %collective-permute-start.5 = (bf16[48,320]{1,0:T(8,128)(2,1)S(1)}, bf16[48,320]{1,0:T(8,128)(2,1)S(1)}, u32[]{:S(2)}, u32[]{:S(2)}) collective-permute-start(bf16[48,320]{1,0:T(8,128)(2,1)S(1)} %pad_maximum_fusion.3), channel_id=1, source_target_pairs={{0,192},{32,224},{64,0},{96,32},{128,64},{160,96},{192,128},{224,1... | collective-permute-start | bytes 92168 | tf_op jit(solution)/shard_map/ppermute | solution.py:79
  32.6 2.9 collective-permute-start.6
  33.4 5.8 %collective-permute-start.11 = (s32[512]{0:T(512)}, s32[512]{0:T(512)S(1)}, u32[]{:S(2)}, u32[]{:S(2)}) collective-permute-start(s32[512]{0:T(512)} %param.19), channel_id=1, source_target_pairs={{0,8},{8,0},{1,9},{9,1},{2,10},{10,2},{3,11},{11,3},{4,12},{12,4},... | collective-permute-start | bytes 6152 | tf_op jit(solution)/shard_map/ppermute | solution.py:135
  36.2 27.7 %collective-permute-start.7 = (bf16[8,48,320]{2,1,0:T(8,128)(2,1)S(1)}, bf16[8,48,320]{2,1,0:T(8,128)(2,1)S(1)}, u32[]{:S(2)}, u32[]{:S(2)}) collective-permute-start(bf16[8,48,320]{2,1,0:T(8,128)(2,1)S(1)} %broadcast_select_fusion), channel_id=1, source_target_pairs={{0,16},{16,0},{1,17},{17,1},{2,18},{18,2},{3,19},{19,3},{4,20},{20... | collective-permute-start | bytes 737288 | tf_op jit(solution)/shard_map/ppermute | solution.py:83
  64.1 2.4 collective-permute-start.8
  72.3 4.3 %copy-start.3 = (bf16[8,2,2,48,320]{4,3,2,1,0:T(8,128)(2,1)S(1)}, bf16[8,2,2,48,320]{4,3,2,1,0:T(8,128)(2,1)}, u32[]{:S(2)}) copy-start(bf16[8,2,2,48,320]{4,3,2,1,0:T(8,128)(2,1)} %copy.50) | copy-start | bytes 2949124
  77.5 1.4 collective-permute-start.9
  86.0 80.0 %copy-start.5 = (f32[512,8]{0,1:T(8,128)S(1)}, f32[512,8]{0,1:T(8,128)}, u32[]{:S(2)}) copy-start(f32[512,8]{0,1:T(8,128)} %param.26) | copy-start | bytes 49156
  86.0 80.0 %copy-start.6 = (s32[512,8]{0,1:T(8,128)S(1)}, s32[512,8]{0,1:T(8,128)}, u32[]{:S(2)}) copy-start(s32[512,8]{0,1:T(8,128)} %param.25) | copy-start | bytes 49156
  86.0 179.6 %all-reduce.6.cloned.1.call-start = ((), (), s32[]{:S(2)}) async-start(), calls=%async_computation.5 | async-start | bytes 6291456 | tf_op jit(solution)/shard_map/psum | solution.py:13
  165.7 162.0 %reduce-scatter.4.cloned.1.call-start = ((), (), s32[]{:S(2)}) async-start(), calls=%async_computation.6 | async-start | bytes 1769472
  268.1 7.6 %copy-start.2 = (bf16[512,1536]{1,0:T(8,128)(2,1)}, bf16[512,1536]{1,0:T(8,128)(2,1)S(1)}, u32[]{:S(2)}) copy-start(bf16[512,1536]{1,0:T(8,128)(2,1)S(1)} %get-tuple-element.47) | copy-start | bytes 4718596
  268.1 7.5 %copy-start.8 = (bf16[5,256,1536]{2,1,0:T(8,128)(2,1)S(1)}, bf16[5,256,1536]{2,1,0:T(8,128)(2,1)}, u32[]{:S(2)}) copy-start(bf16[5,256,1536]{2,1,0:T(8,128)(2,1)} %param.28) | copy-start | bytes 11796484
  279.1 1.6 copy-start.1
  288.8 19.3 %all-to-all-start = ((s32[32,1,16]{2,1,0:T(1,128)}), s32[32,1,16]{2,1,0:T(1,128)S(1)}, u32[]{:S(2)}, u32[]{:S(2)}) async-start(s32[32,1,16]{2,1,0:T(1,128)} %bitcast.32), calls=%async_computation | async-start | bytes 32768 | tf_op jit(solution)/shard_map/all_to_all | solution.py:168
  310.2 15.1 %all-to-all-start.1 = ((bf16[32,16,1,128]{3,1,2,0:T(8,128)(2,1)}), bf16[32,16,1,128]{3,1,2,0:T(8,128)(2,1)S(1)}, u32[]{:S(2)}, u32[]{:S(2)}) async-start(bf16[32,16,1,128]{3,1,2,0:T(8,128)(2,1)} %bitcast.36), calls=%async_computation.1 | async-start | bytes 262144 | tf_op jit(solution)/shard_map/all_to_all | solution.py:167
Sparse Core Ops, SparseCore 0:
  21.1 40.3 all-gather.1
  86.1 79.4 all-reduce.3
  168.2 97.3 all-reduce.5
  280.9 39.8 reduce-scatter.3
